TPU v7x, 32 devices: a whole 2x2x4 slice. The times are simulated.
32 devices in a mesh: dp: 16 (over z, y, core), tensor: 2 (over x).
Axes of the slice: x: 2, y: 2, z: 4, core: 2. Of those that a mesh axis runs over, the one named last changes fastest.
Arguments:
- hidden_states: bfloat16 [8192, 2048], P('dp', 'tensor'), may hold values from -6 to 6
- norm_gain: bfloat16 [2048], replicated, may hold values from 0.25 to 1.75
- head_weight: bfloat16 [2048, 25600], P(None, ('tensor', 'dp')), may hold values from -1 to 1
- target_ids: int32 [8192], P('dp'), may hold values from 0 to 25599
- loss_mask: int32 [8192], P('dp'), may hold values from 0 to 1, as said below
- seq_lengths: int32 [16], replicated, may hold values from 1 to 4096, as said below
- slot_order: int32 [16], replicated, may hold values from 0 to 15, each once
Outputs:
- token_logprob: float32 [8192], P(('dp', 'tensor'))
- token_entropy: float32 [8192], P(('dp', 'tensor'))
- seq_mean_logprob: float32 [16], P('dp')
- seq_mean_entropy: float32 [16], P('dp')
Inputs may be any that keep to these rules, and one draw needn't show every extreme that they name: `seq_lengths`: sequences lie in packed order, one after another; their lengths sum to 8192; the longest has exactly 4096 tokens and some sequence has exactly 1 token. `slot_order`: each sequence appears once. `loss_mask`: some sequence of exactly 1 token has no scored row.
All inputs are finite; a program needn't handle non-finite values.
Results may differ from a plain program's by a relative error of at most 0.0012.
Values may be sent and summed in bfloat16 or wider, within the bound.
No kernel may reach another device: no remote copies, remote signals or barrier semaphores. Data moves between devices by JAX's collectives and lax.ppermute only.
A program may use at most 192 MiB of HBM per device.

v0:
```python
import jax
import jax.numpy as jnp
from jax import lax
from jax.sharding import PartitionSpec as P

EPS = 1e-05


def per_device(
    hidden_states, norm_gain, head_weight, target_ids, loss_mask, seq_lengths, slot_order
):
    whole = lax.all_gather(hidden_states, "tensor", axis=1, tiled=True)
    values = whole.astype(jnp.float32)
    square = jnp.mean(values * values, axis=1, keepdims=True)
    normed = (values * lax.rsqrt(square + EPS) * norm_gain.astype(jnp.float32)).astype(jnp.bfloat16)
    rows = whole.shape[0]
    groups = lax.axis_size("tensor")
    share = rows // groups
    column_base = lax.axis_index("tensor") * (head_weight.shape[1] * lax.axis_size("dp"))
    piece = lax.all_gather(head_weight, "dp", axis=1, tiled=True)
    top = jnp.full((rows,), -1e30, jnp.float32)
    total = jnp.zeros((rows,), jnp.float32)
    logits = jnp.dot(normed, piece, preferred_element_type=jnp.float32)
    columns = column_base + lax.broadcasted_iota(jnp.int32, (1, piece.shape[1]), 1)
    new_top = jnp.maximum(top, jnp.max(logits, axis=1))
    shifted = logits - new_top[:, None]
    expo = jnp.exp(shifted)
    scale = jnp.exp(top - new_top)
    new_total = jnp.sum(expo, axis=1)
    new_spread = scale * (total * (top - new_top)) + jnp.sum(expo * shifted, axis=1)
    hit = jnp.sum(jnp.where(columns == target_ids[:, None], logits, 0.0), axis=1)
    mine = lax.axis_index("tensor") * share
    row_top = lax.pmax(new_top, "tensor")
    scale = jnp.exp(new_top - row_top)
    sums = lax.psum(
        (new_total * scale, scale * (new_spread + new_total * (new_top - row_top)), hit), "tensor"
    )
    row_top = lax.dynamic_slice_in_dim(row_top, mine, share)
    row_total = lax.dynamic_slice_in_dim(sums[0], mine, share)
    row_spread = lax.dynamic_slice_in_dim(sums[1], mine, share)
    row_picked = lax.dynamic_slice_in_dim(sums[2], mine, share)
    logsum = jnp.log(row_total)
    live = lax.dynamic_slice_in_dim(loss_mask, mine, share).astype(jnp.float32)
    token_logprob = (row_picked - row_top - logsum) * live
    token_entropy = (logsum - row_spread / row_total) * live
    ends = jnp.cumsum(seq_lengths)
    position = lax.axis_index("dp") * rows + mine + jnp.arange(share, dtype=jnp.int32)
    segment = jnp.sum((position[:, None] >= ends[None, :]).astype(jnp.int32), axis=1)
    member = (segment[:, None] == slot_order[None, :]).astype(jnp.float32)
    lp_part = jnp.dot(token_logprob, member, precision=lax.Precision.HIGHEST)
    ent_part = jnp.dot(token_entropy, member, precision=lax.Precision.HIGHEST)
    count_part = jnp.dot(live, member, precision=lax.Precision.HIGHEST)
    lp_sum, ent_sum, count = lax.psum((lp_part, ent_part, count_part), ("dp", "tensor"))
    owned = lp_sum.shape[0] // lax.axis_size("dp")
    first_slot = lax.axis_index("dp") * owned
    floor = jnp.maximum(lax.dynamic_slice_in_dim(count, first_slot, owned), 1.0)
    seq_mean_logprob = lax.dynamic_slice_in_dim(lp_sum, first_slot, owned) / floor
    seq_mean_entropy = lax.dynamic_slice_in_dim(ent_sum, first_slot, owned) / floor
    return (token_logprob, token_entropy, seq_mean_logprob, seq_mean_entropy)


def solution(mesh):
    placed = (P("dp", "tensor"), P(), P(None, ("tensor", "dp")), P("dp"), P("dp"), P(), P())
    return jax.shard_map(
        per_device,
        mesh=mesh,
        in_specs=placed,
        out_specs=(P(("dp", "tensor")), P(("dp", "tensor")), P("dp"), P("dp")),
        check_vma=False,
    )
```

profile of v0, /device:TPU:0, one launch (start us, length us, event | category | flops | bytes accessed | tf_op | source)
XLA Modules:
  0.0 416.9 jit_solution(15467861116896965682)
XLA Ops:
  7.2 0.0 all-gather.3.cloned.1.call-start
  7.2 0.7 all-gather.3.cloned.1.call-update
  7.9 0.0 all-gather.5.cloned.1.call-start
  7.9 0.7 all-gather.5.cloned.1.call-update
  8.7 0.7 convert_element_type.17
  9.3 0.7 copy.13
  10.1 0.1 reduce
  10.2 0.1 convert_reduce_fusion
  10.3 35.1 %all-gather.3.cloned.1.call-done = bf16[512,2048]{1,0:T(8,128)(2,1)} async-done(((bf16[512,1024]{1,0:T(8,128)(2,1)}), bf16[512,2048]{1,0:T(8,128)(2,1)}) %all-gather.3.cloned.1.call-update) | async-done | bytes 2097168 | tf_op jit(solution)/shard_map/all_gather | solution.py:12
  45.4 2.1 fusion.1
  47.5 256.5 %all-gather.5.cloned.1.call-done = bf16[2048,12800]{0,1:T(8,128)(2,1)} async-done(((bf16[2048,800]{0,1:T(8,128)(2,1)}), bf16[2048,12800]{0,1:T(8,128)(2,1)}) %all-gather.5.cloned.1.call-update) | async-done | bytes 52428816 | tf_op jit(solution)/shard_map/all_gather | solution.py:20
  304.0 35.8 %fusion.17 = (f32[512]{0:T(512)S(1)}, f32[512,12800]{1,0:T(8,128)}) fusion(bf16[2048,12800]{0,1:T(8,128)(2,1)} %all-gather.5.cloned.1.call-done, bf16[512,2048]{1,0:T(8,128)(2,1)} %all-gather.3.cloned.1.call-done, f32[2048]{0:T(1024)S(1)} %convert_element_type.17, f32[512]{0:T(512)S(1)} %add_rsqrt_fusion), kind=kOutput, calls=%fused_computation.34 | convolution fusion | flops 26854293504 | bytes 80752640 | tf_op jit(solution)/shard_map/dot_general | solution.py:23
  339.9 4.9 %pmax.7 = f32[512]{0:T(512)S(1)} all-reduce(f32[512]{0:T(512)S(1)} %broadcast_maximum_fusion), channel_id=1, replica_groups=mesh['dp'=16,'tensor'=2] {'tensor'}, use_global_device_ids=true, to_apply=%region_4.5 | all-reduce | flops 512 | bytes 4096 | tf_op jit(solution)/shard_map/pmax | solution.py:33
  344.8 13.5 %fusion = (f32[512]{0:T(512)S(1)}, f32[512]{0:T(512)S(1)}, f32[512]{0:T(512)S(1)}) fusion(f32[512,12800]{1,0:T(8,128)} %get-tuple-element.18, f32[512]{0:T(512)S(1)} %broadcast_maximum_fusion, s32[512]{0:T(512)S(1)} %copy-done, s32[12800]{0:T(1024)S(1)} %iota_add_fusion), kind=kLoop, calls=%fused_computation.2 | loop fusion | flops 45873664 | bytes 26275840 | tf_op jit(solution)/shard_map/reduce_sum | solution.py:30
  358.3 5.0 %all-reduce.1 = (f32[512]{0:T(512)S(1)}, f32[512]{0:T(512)S(1)}, f32[512]{0:T(512)S(1)}) all-reduce(f32[512]{0:T(512)S(1)} %get-tuple-element.6, f32[512]{0:T(512)S(1)} %get-tuple-element.16, f32[512]{0:T(512)S(1)} %get-tuple-element.15), channel_id=1, replica_groups=mesh['dp'=16,'tensor'=2] {'tensor'}, use_global_device_ids=true, to_apply=%region_2.0 | all-reduce | flops 1536 | bytes 12288 | tf_op jit(solution)/shard_map/psum | solution.py:35
  363.3 0.1 subtract_multiply_fusion
  363.4 0.2 convolution_bitcast_fusion
  363.6 0.2 convolution_bitcast_fusion.1
  363.9 0.1 subtract_multiply_fusion.1
  364.0 0.2 convolution_bitcast_fusion.2
  364.2 39.7 %all-reduce = (f32[16]{0:T(128)S(1)}, f32[16]{0:T(128)S(1)}, f32[16]{0:T(128)S(1)}) all-reduce(f32[16]{0:T(128)S(1)} %convolution_bitcast_fusion.2, f32[16]{0:T(128)S(1)} %convolution_bitcast_fusion.1, f32[16]{0:T(128)S(1)} %convolution_bitcast_fusion), channel_id=1, replica_groups=mesh['dp'=16,'tensor'=2] {'dp','tensor'}, use_global_device_ids=true, to_apply=%region_11.12 | all-reduce | flops 48 | bytes 384 | tf_op jit(solution)/shard_map/psum | solution.py:53
  403.9 0.7 dynamic_slice.31
  404.6 0.6 dynamic_slice.30
  405.2 0.6 dynamic_slice.29
  (16 shorter events, 0.1 us)
Async XLA Ops:
  7.2 38.3 %all-gather.3.cloned.1.call-start = ((), (), s32[]{:S(2)}) async-start(), calls=%async_computation | async-start | bytes 3145728 | tf_op jit(solution)/shard_map/all_gather | solution.py:12
  7.9 296.1 %all-gather.5.cloned.1.call-start = ((), (), s32[]{:S(2)}) async-start(), calls=%async_computation.1 | async-start | bytes 55705600 | tf_op jit(solution)/shard_map/all_gather | solution.py:20
  47.5 297.3 %copy-start = (s32[512]{0:T(512)S(1)}, s32[512]{0:T(512)}, u32[]{:S(2)}) copy-start(s32[512]{0:T(512)} %param.10) | copy-start | bytes 6148
  339.9 23.5 %copy-start.3 = (s32[512]{0:T(512)S(1)}, s32[512]{0:T(512)}, u32[]{:S(2)}) copy-start(s32[512]{0:T(512)} %param.11) | copy-start | bytes 6148
  339.9 23.6 %copy-start.4 = (s32[16]{0:T(128)S(1)}, s32[16]{0:T(128)}, u32[]{:S(2)}) copy-start(s32[16]{0:T(128)} %param.13) | copy-start | bytes 196
  363.4 44.3 %copy-start.1 = (f32[256]{0:T(256)}, f32[256]{0:T(256)S(1)}, u32[]{:S(2)}) copy-start(f32[256]{0:T(256)S(1)} %get-tuple-element.13) | copy-start | bytes 3076
  364.0 43.8 %copy-start.2 = (f32[256]{0:T(256)}, f32[256]{0:T(256)S(1)}, u32[]{:S(2)}) copy-start(f32[256]{0:T(256)S(1)} %subtract_multiply_fusion.1) | copy-start | bytes 3076
Sparse Core Ops, SparseCore 0:
  9.5 35.8 all-gather.2
  47.0 256.9 all-gather.4
where the time goes:
time: 417 us
  waiting for transfers between devices  293 us (70%)
  blocking collectives  49.7 us (12%)
  matrix products  36.5 us (9%)
  between operations  18.3 us (4%)
  other arithmetic  16.7 us (4%)
    all_gather x1, waiting for transfers between devices, per_device(): piece = lax.all_gather(head_weight, 'dp', axis=1, tiled=True)  257 us
    psum x1, blocking collectives, per_device(): lax.psum((lp_part, ent_part, count_part), ('dp', 'tensor'))  39.7 us
    dot_general x1, matrix products, per_device(): logits = jnp.dot(normed, piece, preferred_element_type=jnp.float32)  35.8 us
    all_gather x1, waiting for transfers between devices, per_device(): whole = lax.all_gather(hidden_states, 'tensor', axis=1, tiled=True)  35.1 us
    reduce_sum x1, other arithmetic, per_device(): jnp.sum(expo * shifted, axis=1)  13.5 us
  transfers between devices with their start and end apart: 2, of which 2 were waited for; matrix products, arithmetic and copies ran while one was open for 1% of the time, Pallas kernels for 0%

commit v1 on v0

--- a/solution.py
+++ b/solution.py
@@ -17,7 +17,27 @@
     groups = lax.axis_size("tensor")
     share = rows // groups
     column_base = lax.axis_index("tensor") * (head_weight.shape[1] * lax.axis_size("dp"))
-    piece = lax.all_gather(head_weight, "dp", axis=1, tiled=True)
+    local_now, aux, w2 = (jax.lax.axis_size("dp"), jax.lax.axis_index("dp"), head_weight.shape[1])
+    piece = lax.dynamic_update_slice_in_dim(
+        jnp.zeros(
+            tuple((num * local_now if p == 1 else num for p, num in enumerate(head_weight.shape))),
+            head_weight.dtype,
+        ),
+        head_weight,
+        aux * w2,
+        axis=1,
+    )
+    high = r2 = head_weight
+    for t in range(1, local_now // 2 + 1):
+        high = jax.lax.ppermute(
+            high, "dp", tuple(((p, (p + 1) % local_now) for p in range(local_now)))
+        )
+        piece = lax.dynamic_update_slice_in_dim(piece, high, (aux - t) % local_now * w2, axis=1)
+        if 2 * t < local_now:
+            r2 = jax.lax.ppermute(
+                r2, "dp", tuple(((p, (p - 1) % local_now) for p in range(local_now)))
+            )
+            piece = lax.dynamic_update_slice_in_dim(piece, r2, (aux + t) % local_now * w2, axis=1)
     top = jnp.full((rows,), -1e30, jnp.float32)
     total = jnp.zeros((rows,), jnp.float32)
     logits = jnp.dot(normed, piece, preferred_element_type=jnp.float32)

time: 417 us -> 671 us (1.61)
  starting transfers between devices: 0.08 us -> 405 us
  waiting for transfers between devices: 293 us -> 67.7 us
  local copies, waits for them, and re-layouts: 2.58 us -> 68.5 us
  blocking collectives: 49.7 us -> 57.7 us
    ppermute x0 -> x15, starting transfers between devices: none -> 405 us  [the longest x8 400 us: per_device(): jax.lax.ppermute(high, 'dp', tuple(((p, (p + 1) % local_now) for p in ran...]
    all_gather x1 -> x0, waiting for transfers between devices: 257 us -> none  [per_device(): piece = lax.all_gather(head_weight, 'dp', axis=1, tiled=True)]
    ppermute x0 -> x15, waiting for transfers between devices: none -> 67.7 us  [the longest x8 67.7 us: per_device(): jax.lax.ppermute(high, 'dp', tuple(((p, (p + 1) % local_now) for p in ran...]
    dynamic_update_slice x0 -> x16, local copies, waits for them, and re-layouts: none -> 48.9 us  [the longest x8 26.7 us: per_device(): lax.dynamic_update_slice_in_dim(piece, high, (aux - t) % local_now * w2,...]
    all_gather x1, waiting for transfers between devices: 35.1 us -> 0.01 us  [per_device(): whole = lax.all_gather(hidden_states, 'tensor', axis=1, tiled=True)]
    broadcast_in_dim x0 -> x1, local copies, waits for them, and re-layouts: none -> 17 us  [per_device(): jnp.zeros(tuple((num * local_now if p == 1 else num for p, num in enumera...]
    psum x1, blocking collectives: 39.7 us -> 47.6 us  [per_device(): lax.psum((lp_part, ent_part, count_part), ('dp', 'tensor'))]
  transfers between devices with their start and end apart: 2 -> 16, of which waited for: 2 -> 6; matrix products, arithmetic and copies ran while one was open for 1% -> 10% of each run, Pallas kernels for 0% -> 0%
where the time goes in v1:
time: 671 us; the launch traced here: 670 us
  starting transfers between devices  405 us (60%)
  local copies, waits for them, and re-layouts  68.5 us (10%)
  waiting for transfers between devices  67.7 us (10%)
  blocking collectives  57.7 us (9%)
  matrix products  35.7 us (5%)
  between operations  18.4 us (3%)
  other arithmetic  16.9 us (3%)
    ppermute x8, starting transfers between devices, per_device(): jax.lax.ppermute(high, 'dp', tuple(((p, (p + 1) % local_now) for p in ran...  400 us
    ppermute x8, waiting for transfers between devices, per_device(): jax.lax.ppermute(high, 'dp', tuple(((p, (p + 1) % local_now) for p in ran...  67.7 us
    psum x1, blocking collectives, per_device(): lax.psum((lp_part, ent_part, count_part), ('dp', 'tensor'))  47.6 us
    dot_general x1, matrix products, per_device(): logits = jnp.dot(normed, piece, preferred_element_type=jnp.float32)  35 us
    dynamic_update_slice x8, local copies, waits for them, and re-layouts, per_device(): lax.dynamic_update_slice_in_dim(piece, high, (aux - t) % local_now * w2,...  26.7 us
    dynamic_update_slice x7, local copies, waits for them, and re-layouts, per_device(): lax.dynamic_update_slice_in_dim(piece, r2, (aux + t) % local_now * w2, ax...  20.3 us
    broadcast_in_dim x1, local copies, waits for them, and re-layouts, per_device(): jnp.zeros(tuple((num * local_now if p == 1 else num for p, num in enumera...  17 us
    reduce_sum x1, other arithmetic, per_device(): jnp.sum(expo * shifted, axis=1)  13.5 us
  transfers between devices with their start and end apart: 16, of which 6 were waited for; matrix products, arithmetic and copies ran while one was open for 10% of the time, Pallas kernels for 0%

profile of v1, /device:TPU:0, one launch (start us, length us, event | category | flops | bytes accessed | tf_op | source)
XLA Modules:
  0.0 670.2 jit_solution(15362073734753085879)
XLA Ops:
  7.7 5.1 collective-permute-start.1
  12.8 36.6 %collective-permute-done = bf16[2048,800]{0,1:T(8,128)(2,1)S(1)} collective-permute-done((bf16[2048,800]{0,1:T(8,128)(2,1)}, bf16[2048,800]{0,1:T(8,128)(2,1)S(1)}, u32[]{:S(2)}, u32[]{:S(2)}) %collective-permute-start) | collective-permute-done | bytes 3276832 | tf_op jit(solution)/shard_map/ppermute | solution.py:32
  49.4 32.0 %collective-permute-start.2 = (bf16[2048,800]{0,1:T(8,128)(2,1)S(1)}, bf16[2048,800]{0,1:T(8,128)(2,1)S(1)}, u32[]{:S(2)}, u32[]{:S(2)}) collective-permute-start(bf16[2048,800]{0,1:T(8,128)(2,1)S(1)} %collective-permute-done), channel_id=1, source_target_pairs={{0,2},{2,4},{4,6},{6,8},{8,10},{10,12},{12,14},{14,16},{16,18},{18... | collective-permute-start | bytes 9830408 | tf_op jit(solution)/shard_map/ppermute | solution.py:32
  81.4 8.9 %collective-permute-done.2 = bf16[2048,800]{0,1:T(8,128)(2,1)S(1)} collective-permute-done((bf16[2048,800]{0,1:T(8,128)(2,1)S(1)}, bf16[2048,800]{0,1:T(8,128)(2,1)S(1)}, u32[]{:S(2)}, u32[]{:S(2)}) %collective-permute-start.2) | collective-permute-done | bytes 3276832 | tf_op jit(solution)/shard_map/ppermute | solution.py:32
  90.3 63.5 %collective-permute-start.4 = (bf16[2048,800]{0,1:T(8,128)(2,1)S(1)}, bf16[2048,800]{0,1:T(8,128)(2,1)S(1)}, u32[]{:S(2)}, u32[]{:S(2)}) collective-permute-start(bf16[2048,800]{0,1:T(8,128)(2,1)S(1)} %collective-permute-done.2), channel_id=1, source_target_pairs={{0,2},{2,4},{4,6},{6,8},{8,10},{10,12},{12,14},{14,16},{16,18},{18... | collective-permute-start | bytes 9830408 | tf_op jit(solution)/shard_map/ppermute | solution.py:32
  153.8 5.5 collective-permute-done.4
  159.3 67.0 %collective-permute-start.6 = (bf16[2048,800]{0,1:T(8,128)(2,1)S(1)}, bf16[2048,800]{0,1:T(8,128)(2,1)S(1)}, u32[]{:S(2)}, u32[]{:S(2)}) collective-permute-start(bf16[2048,800]{0,1:T(8,128)(2,1)S(1)} %collective-permute-done.4), channel_id=1, source_target_pairs={{0,2},{2,4},{4,6},{6,8},{8,10},{10,12},{12,14},{14,16},{16,18},{18... | collective-permute-start | bytes 9830408 | tf_op jit(solution)/shard_map/ppermute | solution.py:32
  226.4 5.4 collective-permute-done.6
  231.8 67.0 %collective-permute-start.8 = (bf16[2048,800]{0,1:T(8,128)(2,1)S(1)}, bf16[2048,800]{0,1:T(8,128)(2,1)}, u32[]{:S(2)}, u32[]{:S(2)}) collective-permute-start(bf16[2048,800]{0,1:T(8,128)(2,1)S(1)} %collective-permute-done.6), channel_id=1, source_target_pairs={{0,2},{2,4},{4,6},{6,8},{8,10},{10,12},{12,14},{14,16},{16,18},{18... | collective-permute-start | bytes 9830408 | tf_op jit(solution)/shard_map/ppermute | solution.py:32
  298.9 5.5 collective-permute-done.8
  304.4 65.6 %collective-permute-start.10 = (bf16[2048,800]{0,1:T(8,128)(2,1)}, bf16[2048,800]{0,1:T(8,128)(2,1)}, u32[]{:S(2)}, u32[]{:S(2)}) collective-permute-start(bf16[2048,800]{0,1:T(8,128)(2,1)} %collective-permute-done.8), channel_id=1, source_target_pairs={{0,2},{2,4},{4,6},{6,8},{8,10},{10,12},{12,14},{14,16},{16,18},{18... | collective-permute-start | bytes 9830408 | tf_op jit(solution)/shard_map/ppermute | solution.py:32
  370.0 5.8 collective-permute-done.10
  375.8 66.9 %collective-permute-start.12 = (bf16[2048,800]{0,1:T(8,128)(2,1)}, bf16[2048,800]{0,1:T(8,128)(2,1)}, u32[]{:S(2)}, u32[]{:S(2)}) collective-permute-start(bf16[2048,800]{0,1:T(8,128)(2,1)} %collective-permute-done.10), channel_id=1, source_target_pairs={{0,2},{2,4},{4,6},{6,8},{8,10},{10,12},{12,14},{14,16},{16,18},{18... | collective-permute-start | bytes 9830408 | tf_op jit(solution)/shard_map/ppermute | solution.py:32
  444.5 17.0 %broadcast_in_dim.10 = bf16[2048,12800]{0,1:T(8,128)(2,1)} broadcast(bf16[]{:T(256)} %constant.110.clone.1), dimensions={} | broadcast | bytes 52428800 | tf_op jit(solution)/shard_map/broadcast_in_dim | solution.py:22
  465.7 4.8 constant_dynamic-update-slice_fusion.14
  470.5 4.1 constant_dynamic-update-slice_fusion.13
  478.6 37.6 %collective-permute-start.14 = (bf16[2048,800]{0,1:T(8,128)(2,1)}, bf16[2048,800]{0,1:T(8,128)(2,1)S(1)}, u32[]{:S(2)}, u32[]{:S(2)}) collective-permute-start(bf16[2048,800]{0,1:T(8,128)(2,1)} %collective-permute-done.12), channel_id=1, source_target_pairs={{0,2},{2,4},{4,6},{6,8},{8,10},{10,12},{12,14},{14,16},{16,18},{18... | collective-permute-start | bytes 9830408 | tf_op jit(solution)/shard_map/ppermute | solution.py:32
  530.2 4.1 constant_dynamic-update-slice_fusion.5
  538.2 4.1 constant_dynamic-update-slice_fusion.3
  550.3 35.0 %fusion.17 = (f32[512]{0:T(512)S(1)}, f32[512,12800]{1,0:T(8,128)}) fusion(bf16[2048,12800]{0,1:T(8,128)(2,1)} %constant_dynamic-update-slice_fusion, bf16[512,2048]{1,0:T(8,128)(2,1)S(1)} %copy-done.12, f32[2048]{0:T(1024)S(1)} %convert_element_type.17, f32[512]{0:T(512)S(1)} %add_rsqrt_fusion), kind=kOutput, calls=%fused_computation.50 | convolution fusion | flops 26854293504 | bytes 80752640 | tf_op jit(solution)/shard_map/dot_general | solution.py:43
  585.3 5.1 pmax.7
  590.4 13.5 %fusion = (f32[512]{0:T(512)S(1)}, f32[512]{0:T(512)S(1)}, f32[512]{0:T(512)S(1)}) fusion(f32[512,12800]{1,0:T(8,128)} %get-tuple-element.18, f32[512]{0:T(512)S(1)} %broadcast_maximum_fusion, s32[512]{0:T(512)S(1)} %copy-done.13, s32[12800]{0:T(1024)S(1)} %iota_add_fusion), kind=kLoop, calls=%fused_computation.2 | loop fusion | flops 45873664 | bytes 26275840 | tf_op jit(solution)/shard_map/reduce_sum | solution.py:50
  603.9 5.0 all-reduce.1
  609.8 47.6 %all-reduce = (f32[16]{0:T(128)S(1)}, f32[16]{0:T(128)S(1)}, f32[16]{0:T(128)S(1)}) all-reduce(f32[16]{0:T(128)S(1)} %convolution_bitcast_fusion.2, f32[16]{0:T(128)S(1)} %convolution_bitcast_fusion.1, f32[16]{0:T(128)S(1)} %convolution_bitcast_fusion), channel_id=1, replica_groups=mesh['dp'=16,'tensor'=2] {'dp','tensor'}, use_global_device_ids=true, to_apply=%region_11.12 | all-reduce | flops 48 | bytes 384 | tf_op jit(solution)/shard_map/psum | solution.py:73
  (86 shorter events, 39.2 us)
Async XLA Ops:
  7.2 456.3 %all-gather.2.cloned.1.call-start = ((), (), s32[]{:S(2)}) async-start(), calls=%async_computation | async-start | bytes 3145728 | tf_op jit(solution)/shard_map/all_gather | solution.py:12
  7.2 42.2 %collective-permute-start = (bf16[2048,800]{0,1:T(8,128)(2,1)}, bf16[2048,800]{0,1:T(8,128)(2,1)S(1)}, u32[]{:S(2)}, u32[]{:S(2)}) collective-permute-start(bf16[2048,800]{0,1:T(8,128)(2,1)} %param.9), channel_id=1, source_target_pairs={{0,2},{2,4},{4,6},{6,8},{8,10},{10,12},{12,14},{14,16},{16,18},{18... | collective-permute-start | bytes 9830408 | tf_op jit(solution)/shard_map/ppermute | solution.py:32
  7.7 73.7 %collective-permute-start.1 = (bf16[2048,800]{0,1:T(8,128)(2,1)}, bf16[2048,800]{0,1:T(8,128)(2,1)S(1)}, u32[]{:S(2)}, u32[]{:S(2)}) collective-permute-start(bf16[2048,800]{0,1:T(8,128)(2,1)} %param.9), channel_id=1, source_target_pairs={{0,30},{2,0},{4,2},{6,4},{8,6},{10,8},{12,10},{14,12},{16,14},{18,... | collective-permute-start | bytes 9830408 | tf_op jit(solution)/shard_map/ppermute | solution.py:37
  49.4 40.9 %collective-permute-start.2 = (bf16[2048,800]{0,1:T(8,128)(2,1)S(1)}, bf16[2048,800]{0,1:T(8,128)(2,1)S(1)}, u32[]{:S(2)}, u32[]{:S(2)}) collective-permute-start(bf16[2048,800]{0,1:T(8,128)(2,1)S(1)} %collective-permute-done), channel_id=1, source_target_pairs={{0,2},{2,4},{4,6},{6,8},{8,10},{10,12},{12,14},{14,16},{16,18},{18... | collective-permute-start | bytes 9830408 | tf_op jit(solution)/shard_map/ppermute | solution.py:32
  81.4 72.4 %copy-start.7 = (bf16[2048,800]{0,1:T(8,128)(2,1)}, bf16[2048,800]{0,1:T(8,128)(2,1)S(1)}, u32[]{:S(2)}) copy-start(bf16[2048,800]{0,1:T(8,128)(2,1)S(1)} %collective-permute-done.1) | copy-start | bytes 9830404
  81.4 72.4 %collective-permute-start.3 = (bf16[2048,800]{0,1:T(8,128)(2,1)S(1)}, bf16[2048,800]{0,1:T(8,128)(2,1)S(1)}, u32[]{:S(2)}, u32[]{:S(2)}) collective-permute-start(bf16[2048,800]{0,1:T(8,128)(2,1)S(1)} %collective-permute-done.1), channel_id=1, source_target_pairs={{0,30},{2,0},{4,2},{6,4},{8,6},{10,8},{12,10},{14,12},{16,14},{18,... | collective-permute-start | bytes 9830408 | tf_op jit(solution)/shard_map/ppermute | solution.py:37
  90.3 141.5 %copy-start.3 = (bf16[2048,800]{0,1:T(8,128)(2,1)}, bf16[2048,800]{0,1:T(8,128)(2,1)S(1)}, u32[]{:S(2)}) copy-start(bf16[2048,800]{0,1:T(8,128)(2,1)S(1)} %collective-permute-done.2) | copy-start | bytes 9830404
  90.3 69.0 %collective-permute-start.4 = (bf16[2048,800]{0,1:T(8,128)(2,1)S(1)}, bf16[2048,800]{0,1:T(8,128)(2,1)S(1)}, u32[]{:S(2)}, u32[]{:S(2)}) collective-permute-start(bf16[2048,800]{0,1:T(8,128)(2,1)S(1)} %collective-permute-done.2), channel_id=1, source_target_pairs={{0,2},{2,4},{4,6},{6,8},{8,10},{10,12},{12,14},{14,16},{16,18},{18... | collective-permute-start | bytes 9830408 | tf_op jit(solution)/shard_map/ppermute | solution.py:32
  153.8 72.4 %collective-permute-start.5 = (bf16[2048,800]{0,1:T(8,128)(2,1)S(1)}, bf16[2048,800]{0,1:T(8,128)(2,1)S(1)}, u32[]{:S(2)}, u32[]{:S(2)}) collective-permute-start(bf16[2048,800]{0,1:T(8,128)(2,1)S(1)} %collective-permute-done.3), channel_id=1, source_target_pairs={{0,30},{2,0},{4,2},{6,4},{8,6},{10,8},{12,10},{14,12},{16,14},{18,... | collective-permute-start | bytes 9830408 | tf_op jit(solution)/shard_map/ppermute | solution.py:37
  159.3 67.0 %copy-start.1 = (bf16[2048,800]{0,1:T(8,128)(2,1)}, bf16[2048,800]{0,1:T(8,128)(2,1)S(1)}, u32[]{:S(2)}) copy-start(bf16[2048,800]{0,1:T(8,128)(2,1)S(1)} %collective-permute-done.4) | copy-start | bytes 9830404
  159.3 72.4 %collective-permute-start.6 = (bf16[2048,800]{0,1:T(8,128)(2,1)S(1)}, bf16[2048,800]{0,1:T(8,128)(2,1)S(1)}, u32[]{:S(2)}, u32[]{:S(2)}) collective-permute-start(bf16[2048,800]{0,1:T(8,128)(2,1)S(1)} %collective-permute-done.4), channel_id=1, source_target_pairs={{0,2},{2,4},{4,6},{6,8},{8,10},{10,12},{12,14},{14,16},{16,18},{18... | collective-permute-start | bytes 9830408 | tf_op jit(solution)/shard_map/ppermute | solution.py:32
  226.3 72.5 %copy-start.4 = (bf16[2048,800]{0,1:T(8,128)(2,1)}, bf16[2048,800]{0,1:T(8,128)(2,1)S(1)}, u32[]{:S(2)}) copy-start(bf16[2048,800]{0,1:T(8,128)(2,1)S(1)} %collective-permute-done.5) | copy-start | bytes 9830404
  226.3 72.5 %collective-permute-start.7 = (bf16[2048,800]{0,1:T(8,128)(2,1)S(1)}, bf16[2048,800]{0,1:T(8,128)(2,1)S(1)}, u32[]{:S(2)}, u32[]{:S(2)}) collective-permute-start(bf16[2048,800]{0,1:T(8,128)(2,1)S(1)} %collective-permute-done.5), channel_id=1, source_target_pairs={{0,30},{2,0},{4,2},{6,4},{8,6},{10,8},{12,10},{14,12},{16,14},{18,... | collective-permute-start | bytes 9830408 | tf_op jit(solution)/shard_map/ppermute | solution.py:37
  231.8 67.0 %copy-start.8 = (bf16[2048,800]{0,1:T(8,128)(2,1)}, bf16[2048,800]{0,1:T(8,128)(2,1)S(1)}, u32[]{:S(2)}) copy-start(bf16[2048,800]{0,1:T(8,128)(2,1)S(1)} %collective-permute-done.6) | copy-start | bytes 9830404
  231.8 72.6 %collective-permute-start.8 = (bf16[2048,800]{0,1:T(8,128)(2,1)S(1)}, bf16[2048,800]{0,1:T(8,128)(2,1)}, u32[]{:S(2)}, u32[]{:S(2)}) collective-permute-start(bf16[2048,800]{0,1:T(8,128)(2,1)S(1)} %collective-permute-done.6), channel_id=1, source_target_pairs={{0,2},{2,4},{4,6},{6,8},{8,10},{10,12},{12,14},{14,16},{16,18},{18... | collective-permute-start | bytes 9830408 | tf_op jit(solution)/shard_map/ppermute | solution.py:32
  298.8 71.1 %collective-permute-start.9 = (bf16[2048,800]{0,1:T(8,128)(2,1)S(1)}, bf16[2048,800]{0,1:T(8,128)(2,1)}, u32[]{:S(2)}, u32[]{:S(2)}) collective-permute-start(bf16[2048,800]{0,1:T(8,128)(2,1)S(1)} %collective-permute-done.7), channel_id=1, source_target_pairs={{0,30},{2,0},{4,2},{6,4},{8,6},{10,8},{12,10},{14,12},{16,14},{18,... | collective-permute-start | bytes 9830408 | tf_op jit(solution)/shard_map/ppermute | solution.py:37
  304.4 71.4 %collective-permute-start.10 = (bf16[2048,800]{0,1:T(8,128)(2,1)}, bf16[2048,800]{0,1:T(8,128)(2,1)}, u32[]{:S(2)}, u32[]{:S(2)}) collective-permute-start(bf16[2048,800]{0,1:T(8,128)(2,1)} %collective-permute-done.8), channel_id=1, source_target_pairs={{0,2},{2,4},{4,6},{6,8},{8,10},{10,12},{12,14},{14,16},{16,18},{18... | collective-permute-start | bytes 9830408 | tf_op jit(solution)/shard_map/ppermute | solution.py:32
  369.9 104.6 %collective-permute-start.11 = (bf16[2048,800]{0,1:T(8,128)(2,1)}, bf16[2048,800]{0,1:T(8,128)(2,1)}, u32[]{:S(2)}, u32[]{:S(2)}) collective-permute-start(bf16[2048,800]{0,1:T(8,128)(2,1)} %collective-permute-done.9), channel_id=1, source_target_pairs={{0,30},{2,0},{4,2},{6,4},{8,6},{10,8},{12,10},{14,12},{16,14},{18,... | collective-permute-start | bytes 9830408 | tf_op jit(solution)/shard_map/ppermute | solution.py:37
  375.8 102.9 %collective-permute-start.12 = (bf16[2048,800]{0,1:T(8,128)(2,1)}, bf16[2048,800]{0,1:T(8,128)(2,1)}, u32[]{:S(2)}, u32[]{:S(2)}) collective-permute-start(bf16[2048,800]{0,1:T(8,128)(2,1)} %collective-permute-done.10), channel_id=1, source_target_pairs={{0,2},{2,4},{4,6},{6,8},{8,10},{10,12},{12,14},{14,16},{16,18},{18... | collective-permute-start | bytes 9830408 | tf_op jit(solution)/shard_map/ppermute | solution.py:32
  463.4 56.9 %copy-start.5 = (bf16[2048,800]{0,1:T(8,128)(2,1)S(1)}, bf16[2048,800]{0,1:T(8,128)(2,1)}, u32[]{:S(2)}) copy-start(bf16[2048,800]{0,1:T(8,128)(2,1)} %copy-done.4) | copy-start | bytes 9830404
  463.4 58.8 %copy-start.9 = (bf16[2048,800]{0,1:T(8,128)(2,1)S(1)}, bf16[2048,800]{0,1:T(8,128)(2,1)}, u32[]{:S(2)}) copy-start(bf16[2048,800]{0,1:T(8,128)(2,1)} %copy-done.8) | copy-start | bytes 9830404
  463.4 60.8 %copy-start.11 = (bf16[2048,800]{0,1:T(8,128)(2,1)S(1)}, bf16[2048,800]{0,1:T(8,128)(2,1)}, u32[]{:S(2)}) copy-start(bf16[2048,800]{0,1:T(8,128)(2,1)} %copy-done.10) | copy-start | bytes 9830404
  474.6 71.8 %collective-permute-start.13 = (bf16[2048,800]{0,1:T(8,128)(2,1)}, bf16[2048,800]{0,1:T(8,128)(2,1)S(1)}, u32[]{:S(2)}, u32[]{:S(2)}) collective-permute-start(bf16[2048,800]{0,1:T(8,128)(2,1)} %collective-permute-done.11), channel_id=1, source_target_pairs={{0,30},{2,0},{4,2},{6,4},{8,6},{10,8},{12,10},{14,12},{16,14},{18,... | collective-permute-start | bytes 9830408 | tf_op jit(solution)/shard_map/ppermute | solution.py:37
  478.6 69.7 %collective-permute-start.14 = (bf16[2048,800]{0,1:T(8,128)(2,1)}, bf16[2048,800]{0,1:T(8,128)(2,1)S(1)}, u32[]{:S(2)}, u32[]{:S(2)}) collective-permute-start(bf16[2048,800]{0,1:T(8,128)(2,1)} %collective-permute-done.12), channel_id=1, source_target_pairs={{0,2},{2,4},{4,6},{6,8},{8,10},{10,12},{12,14},{14,16},{16,18},{18... | collective-permute-start | bytes 9830408 | tf_op jit(solution)/shard_map/ppermute | solution.py:32
  (10 other events, 326.8 us)
Sparse Core Ops, SparseCore 0:
  370.1 69.9 all-gather.1
